TPU v7x, 128 devices: a whole 4x4x4 slice. The times are simulated.
128 devices in a mesh: dp: 16 (over x, y_lo, core), tensor: 8 (over z, y_hi).
Axes of the slice: x: 4, y: 4 (y_hi: 2, y_lo: 2; y = y_hi * 2 + y_lo), z: 4, core: 2. Of those that a mesh axis runs over, the one named last changes fastest.
Arguments:
- rows_in: bfloat16 [2048, 6144], P('dp'), may hold values from -6 to 6
- out_grad: bfloat16 [2048, 6144], P('dp'), may hold values from -1.5 to 1.5
- gate_pre: bfloat16 [2048, 12288], P('dp', 'tensor'), may hold values from -5 to 5
- up_pre: bfloat16 [2048, 12288], P('dp', 'tensor'), may hold values from -5 to 5
- w_gate: bfloat16 [2, 6144, 12288], P(None, 'dp', 'tensor'), may hold values from -0.078125 to 0.078125
- w_up: bfloat16 [2, 6144, 12288], P(None, 'dp', 'tensor'), may hold values from -0.078125 to 0.078125
- w_down: bfloat16 [2, 12288, 6144], P(None, 'tensor', 'dp'), may hold values from -0.0546875 to 0.0546875
- live_rows: int32 [16], P('dp'), may hold values from 32 to 128, as said below
- block_expert: int32 [16], replicated, may hold values from 0 to 1, as said below
Outputs:
- input_grad: bfloat16 [2048, 6144], P('dp', 'tensor')
- grad_gate: bfloat16 [2, 6144, 12288], P(None, 'dp', 'tensor')
- grad_up: bfloat16 [2, 6144, 12288], P(None, 'dp', 'tensor')
- grad_down: bfloat16 [2, 12288, 6144], P(None, 'tensor', 'dp')
Inputs may be any that keep to these rules, and one draw needn't show every extreme that they name: `live_rows`: entry k counts the live rows among rank k's 128 rows; they come first and the rest are padding; some rank is full. `block_expert`: the expert of each aligned block of 128 rows; every expert owns at least one block.
All inputs are finite; a program needn't handle non-finite values.
Results may differ from a plain program's by a relative error of at most 0.005.
Values may be sent and summed in bfloat16 or wider, within the bound.
No kernel may reach another device: no remote copies, remote signals or barrier semaphores. Data moves between devices by JAX's collectives and lax.ppermute only.
A program may use at most 128 MiB of HBM per device.

v0:
```python
import numpy as np
import jax
import jax.numpy as jnp
from jax import lax
from jax.sharding import Mesh
from jax.sharding import PartitionSpec as P

BLOCK = 128
AXES = ("x", "ylo", "core", "z", "yhi")
SIZES = (4, 2, 2, 4, 2)
DP = ("x", "ylo", "core")
TP = ("z", "yhi")
CHIPS = ("x", "ylo")
N_DP = 16
N_TP = 8


def rank_of_pos(pos):
    core, x, ylo = (pos // 8, pos % 8 // 2, pos % 2)
    return x * 4 + ylo * 2 + core


POS_RANK = np.array([rank_of_pos(p) for p in range(N_DP)], np.int32)


def deliver_perm(k):
    pairs = []
    for i in range(N_DP):
        for t in range(N_TP):
            dest = rank_of_pos(2 * t + (i % 2 ^ k))
            pairs.append((i * N_TP + t, dest * N_TP + i // 2))
    return pairs


def contract_rows(left_op, right_op):
    return lax.dot_general(
        left_op, right_op, (((0,), (0,)), ((), ())), preferred_element_type=jnp.float32
    )


def contract_cols(left_op, right_op):
    return lax.dot_general(
        left_op, right_op, (((1,), (1,)), ((), ())), preferred_element_type=jnp.float32
    )


def expert_masks(block_expert, row_count, expert_count):
    spread = jnp.broadcast_to(block_expert[:, None], (row_count // BLOCK, BLOCK)).reshape(
        row_count, 1
    )
    return [(spread == which).astype(jnp.bfloat16) for which in range(expert_count)]


def to_gathered_order(cols):
    width = cols.shape[1]
    return cols.reshape(4, 2, 2, BLOCK, width).transpose(2, 0, 1, 3, 4).reshape(-1, width)


def shards(rows_in, out_grad, gate_pre, up_pre, w_gate, w_up, w_down, live_rows, block_expert):
    rows_dev = rows_in.shape[0]
    expert_count = w_gate.shape[0]
    ff = gate_pre.shape[1]
    dy_cols = to_gathered_order(
        lax.all_to_all(out_grad, DP, split_axis=1, concat_axis=0, tiled=True)
    )
    x_cols = to_gathered_order(lax.all_to_all(rows_in, DP, split_axis=1, concat_axis=0, tiled=True))
    row_count = dy_cols.shape[0]
    expert_g = jnp.take(block_expert, jnp.asarray(POS_RANK), axis=0)
    masks = expert_masks(expert_g, row_count, expert_count)
    positions = jnp.arange(rows_dev, dtype=jnp.int32)[:, None]
    row_mask = (positions < live_rows[0]).astype(jnp.float32)
    gate_vals = gate_pre.astype(jnp.float32)
    up_vals = up_pre.astype(jnp.float32)
    sigmoid = jax.nn.sigmoid(gate_vals)
    silu_vals = gate_vals * sigmoid
    hidden = (silu_vals * up_vals * row_mask).astype(jnp.bfloat16)
    result = jnp.zeros((row_count, ff), jnp.float32)
    for which in range(expert_count):
        result = result + contract_cols(dy_cols * masks[which], w_down[which])
    result = lax.psum_scatter(
        result.reshape(2, row_count // 2, ff), "core", scatter_dimension=0, tiled=True
    ).reshape(row_count // 2, ff)
    hidden_grad = lax.psum_scatter(result, CHIPS, scatter_dimension=0, tiled=True)
    up_grad = (hidden_grad * silu_vals * row_mask).astype(jnp.bfloat16)
    gate_grad = (
        hidden_grad * up_vals * sigmoid * (1.0 + gate_vals * (1.0 - sigmoid)) * row_mask
    ).astype(jnp.bfloat16)
    packed = jnp.stack([hidden, gate_grad, up_grad], axis=1)
    packed = lax.all_gather(packed, CHIPS, axis=0, tiled=True)
    packed = lax.all_gather(packed, "core", axis=0, tiled=True)
    hid_g, gate_g, up_g = (packed[:, 0], packed[:, 1], packed[:, 2])
    down_terms = []
    gate_terms = []
    up_terms = []
    partial_rows = jnp.zeros((row_count, w_gate.shape[1]), jnp.float32)
    for which in range(expert_count):
        down_terms.append(contract_rows(hid_g * masks[which], dy_cols))
        gate_masked = gate_g * masks[which]
        up_masked = up_g * masks[which]
        gate_terms.append(contract_rows(x_cols, gate_masked))
        up_terms.append(contract_rows(x_cols, up_masked))
        partial_rows = (
            partial_rows
            + contract_cols(gate_masked, w_gate[which])
            + contract_cols(up_masked, w_up[which])
        )
    down_total = jnp.stack(down_terms, 0)
    gate_total = jnp.stack(gate_terms, 0)
    up_total = jnp.stack(up_terms, 0)
    width = partial_rows.shape[1]
    summed = lax.psum_scatter(
        partial_rows.reshape(N_TP, row_count // N_TP, width), TP, scatter_dimension=0, tiled=True
    ).reshape(2, rows_dev, width)
    core = lax.axis_index("core")
    ylo = lax.axis_index("ylo")
    got = []
    for k in range(2):
        piece = lax.dynamic_index_in_dim(summed, core ^ k, 0, keepdims=False)
        got.append(lax.ppermute(piece, AXES, deliver_perm(k)))
    first = jnp.where(ylo == 0, got[0], got[1])
    second = jnp.where(ylo == 0, got[1], got[0])
    input_grad = jnp.concatenate([first, second], axis=1).astype(jnp.bfloat16)
    return (
        input_grad,
        gate_total.astype(jnp.bfloat16),
        up_total.astype(jnp.bfloat16),
        down_total.astype(jnp.bfloat16),
    )


def solution(mesh):
    fine = Mesh(mesh.devices.reshape(SIZES), AXES)
    return jax.shard_map(
        shards,
        mesh=fine,
        in_specs=(
            P(DP, None),
            P(DP, None),
            P(DP, TP),
            P(DP, TP),
            P(None, DP, TP),
            P(None, DP, TP),
            P(None, TP, DP),
            P(DP),
            P(),
        ),
        out_specs=(P(DP, TP), P(None, DP, TP), P(None, DP, TP), P(None, TP, DP)),
        check_vma=False,
    )
```

profile of v0, /device:TPU:57, one launch (start us, length us, event | category | flops | bytes accessed | tf_op | source)
XLA Modules:
  0.0 575.7 jit_solution(3465949403237092074)
XLA Ops:
  7.2 2.6 copy.28
  9.8 6.2 %all-to-all-start = ((bf16[128,16,384]{0,2,1:T(8,128)(2,1)}), bf16[128,16,384]{0,2,1:T(8,128)(2,1)S(1)}, u32[]{:S(2)}, u32[]{:S(2)}) async-start(bf16[128,16,384]{0,2,1:T(8,128)(2,1)} %bitcast.2), calls=%async_computation | async-start | bytes 3145728 | tf_op jit(solution)/shard_map/all_to_all | solution.py:64
  16.1 0.7 gather_fusion
  17.2 20.2 %all-to-all-done = bf16[128,16,384]{0,2,1:T(8,128)(2,1)S(1)} async-done(((bf16[128,16,384]{0,2,1:T(8,128)(2,1)}), bf16[128,16,384]{0,2,1:T(8,128)(2,1)S(1)}, u32[]{:S(2)}, u32[]{:S(2)}) %all-to-all-start) | async-done | bytes 1572896 | tf_op jit(solution)/shard_map/all_to_all | solution.py:64
  37.4 0.9 copy.29
  38.2 0.4 broadcast_multiply_fusion
  38.6 0.2 copy.31
  38.8 0.2 copy.33
  39.0 1.4 copy-done.2
  40.5 3.5 fusion.77
  43.9 6.5 %convolution_add_fusion = f32[2048,1536]{1,0:T(8,128)} fusion(f32[2048,1536]{1,0:T(8,128)S(1)} %fusion.77, bf16[2048,384]{1,0:T(8,128)(2,1)S(1)} %bitcast.138, bf16[2,1536,384]{2,1,0:T(8,128)(2,1)S(1)} %copy-done.2), kind=kOutput, calls=%fused_computation.1 | convolution fusion | flops 2419064832 | bytes 27918336 | tf_op jit(solution)/shard_map/dot_general | solution.py:42
  50.6 25.1 %reduce-scatter.4.cloned.1.call-done = f32[1,1024,1536]{2,1,0:T(8,128)} async-done(((f32[2,1024,1536]{2,1,0:T(8,128)}), f32[1,1024,1536]{2,1,0:T(8,128)}) %reduce-scatter.4.cloned.1.call-update) | async-done | bytes 6291472 | tf_op jit(solution)/shard_map/reduce_scatter | solution.py:80
  76.4 131.5 %reduce-scatter.6.cloned.1.call-done = f32[128,1536]{1,0:T(8,128)} async-done(((f32[1024,1536]{1,0:T(8,128)}), f32[128,1536]{1,0:T(8,128)}) %reduce-scatter.6.cloned.1.call-update) | async-done | bytes 786448 | tf_op jit(solution)/shard_map/reduce_scatter | solution.py:83
  208.0 1.7 fusion.97
  209.7 1.1 pad_maximum_fusion.3
  210.9 189.0 %all-gather.3.cloned.1.call-done = bf16[1024,3,1536]{2,0,1:T(8,128)(2,1)} async-done(((bf16[128,3,1536]{2,0,1:T(8,128)(2,1)}), bf16[1024,3,1536]{2,0,1:T(8,128)(2,1)}) %all-gather.3.cloned.1.call-update) | async-done | bytes 9437200 | tf_op jit(solution)/shard_map/all_gather | solution.py:89
  399.9 1.4 copy-done.3
  401.3 1.6 copy.34
  402.9 7.1 %all-to-all-start.1 = ((bf16[128,16,384]{0,2,1:T(8,128)(2,1)}), bf16[128,16,384]{0,2,1:T(8,128)(2,1)S(1)}, u32[]{:S(2)}, u32[]{:S(2)}) async-start(bf16[128,16,384]{0,2,1:T(8,128)(2,1)} %bitcast.142), calls=%async_computation.4 | async-start | bytes 3145728 | tf_op jit(solution)/shard_map/all_to_all | solution.py:66
  410.0 0.5 reduce-scatter.8.cloned.1.call-start
  410.6 28.3 %all-gather.5.cloned.1.call-done = bf16[2048,3,1536]{2,0,1:T(8,128)(2,1)} async-done(((bf16[1024,3,1536]{2,0,1:T(8,128)(2,1)}), bf16[2048,3,1536]{2,0,1:T(8,128)(2,1)}) %all-gather.5.cloned.1.call-update) | async-done | bytes 18874384 | tf_op jit(solution)/shard_map/all_gather | solution.py:90
  438.9 8.3 %fusion.6 = f32[2048,384]{1,0:T(8,128)} fusion(bf16[2048,3,1536]{2,0,1:T(8,128)(2,1)} %all-gather.5.cloned.1.call-done, bf16[2048]{0:T(1024)(128)(2,1)S(1)} %get-tuple-element.31, bf16[2,384,1536]{2,1,0:T(8,128)(2,1)} %param.15), kind=kOutput, calls=%fused_computation.8 | convolution fusion | flops 2419064832 | bytes 10620928 | tf_op jit(solution)/shard_map/dot_general | solution.py:42
  447.3 1.3 copy-done.10
  448.6 0.7 copy-done.11
  449.2 5.2 fusion.14
  454.4 5.2 fusion.18
  459.6 7.3 %add_add_fusion = f32[2048,384]{1,0:T(8,128)} fusion(f32[2048,384]{1,0:T(8,128)} %fusion.6, f32[2048,384]{1,0:T(8,128)} %fusion.18, f32[2048,384]{1,0:T(8,128)} %fusion.14, bf16[2048,3,1536]{2,0,1:T(8,128)(2,1)S(1)} %copy-done.10, bf16[2048]{0:T(1024)(128)(2,1)S(1)} %get-tuple-element.31, bf16[2,384,1536]{2,1,0:T(8,128)(2,1)S(1)} %copy-done.12), kind=kOutput, calls=%fused_computation.30 | convolution fusion | flops 2421424128 | bytes 20058112 | tf_op jit(solution)/shard_map/dot_general | solution.py:42
  466.9 1.6 copy.36
  468.5 1.7 copy.37
  470.2 6.5 %fusion.63 = bf16[1,384,1536]{1,2,0:T(8,128)(2,1)S(1)} fusion(bf16[2048,384]{1,0:T(8,128)(2,1)S(1)} %bitcast.147, bf16[2048,3,1536]{2,0,1:T(8,128)(2,1)} %all-gather.5.cloned.1.call-done, bf16[2048]{0:T(1024)(128)(2,1)S(1)} %get-tuple-element.31), kind=kOutput, calls=%fused_computation.50 | convolution fusion | flops 2419654656 | bytes 9048064 | tf_op jit(solution)/shard_map/dot_general | solution.py:36
  476.8 6.7 %fusion.69 = bf16[1,384,1536]{1,2,0:T(8,128)(2,1)S(1)} fusion(bf16[2048,384]{1,0:T(8,128)(2,1)S(1)} %bitcast.148, bf16[2048,3,1536]{2,0,1:T(8,128)(2,1)} %all-gather.5.cloned.1.call-done, bf16[2048]{0:T(1024)(128)(2,1)S(1)} %get-tuple-element.32), kind=kOutput, calls=%fused_computation.52 | convolution fusion | flops 2419654656 | bytes 9048064 | tf_op jit(solution)/shard_map/dot_general | solution.py:36
  483.5 0.3 pad_maximum_fusion
  483.9 1.1 copy-done.6
  485.0 3.7 fusion.60
  488.6 3.9 fusion.66
  492.6 1.7 pad_maximum_fusion.1
  494.2 0.2 copy-done.4
  494.4 3.7 fusion.54
  498.1 4.7 fusion.57
  502.8 41.4 %reduce-scatter.8.cloned.1.call-done = f32[1,256,384]{2,1,0:T(8,128)} async-done(((f32[8,256,384]{2,1,0:T(8,128)}), f32[1,256,384]{2,1,0:T(8,128)}) %reduce-scatter.8.cloned.1.call-update) | async-done | bytes 393232 | tf_op jit(solution)/shard_map/reduce_scatter | solution.py:111
  544.2 1.7 dynamic-slice_bitcast_fusion.1
  545.9 6.2 %collective-permute-start = (bf16[128,384]{1,0:T(8,128)(2,1)}, bf16[128,384]{1,0:T(8,128)(2,1)}, u32[]{:S(2)}, u32[]{:S(2)}) collective-permute-start(bf16[128,384]{1,0:T(8,128)(2,1)} %get-tuple-element.25), channel_id=1, source_target_pairs={{0,0},{1,32},{2,64},{3,96},{4,8},{5,40},{6,72},{7,104},{8,16},{9,4... | collective-permute-start | bytes 294920 | tf_op jit(solution)/shard_map/ppermute | solution.py:119
  552.1 5.3 collective-permute-start.1
  557.4 2.9 pad_maximum_fusion.2
  560.4 2.6 copy.38
  563.0 4.3 copy.39
  567.2 1.0 select_convert_fusion.1
  568.2 0.7 pad_maximum_fusion.4
  (51 shorter events, 0.8 us)
Async XLA Ops:
  7.2 8.9 %copy-start = (s32[16]{0:T(128)S(1)}, s32[16]{0:T(128)}, u32[]{:S(2)}) copy-start(s32[16]{0:T(128)} %param.18) | copy-start | bytes 196
  9.8 6.3 %copy-start.9 = (s32[16]{0:T(128)S(1)}, s32[16]{0:T(128)}, u32[]{:S(2)}) copy-start(s32[16]{0:T(128)} %constant.52) | copy-start | bytes 196
  9.8 27.6 %all-to-all-start = ((bf16[128,16,384]{0,2,1:T(8,128)(2,1)}), bf16[128,16,384]{0,2,1:T(8,128)(2,1)S(1)}, u32[]{:S(2)}, u32[]{:S(2)}) async-start(bf16[128,16,384]{0,2,1:T(8,128)(2,1)} %bitcast.2), calls=%async_computation | async-start | bytes 3145728 | tf_op jit(solution)/shard_map/all_to_all | solution.py:64
  16.0 59.6 %reduce-scatter.4.cloned.1.call-start = ((), (), s32[]{:S(2)}) async-start(), calls=%async_computation.5 | async-start | bytes 18874368 | tf_op jit(solution)/shard_map/reduce_scatter | solution.py:80
  38.8 1.7 copy-start.2
  50.5 157.4 %reduce-scatter.6.cloned.1.call-start = ((), (), s32[]{:S(2)}) async-start(), calls=%async_computation.6 | async-start | bytes 7077888 | tf_op jit(solution)/shard_map/reduce_scatter | solution.py:83
  75.6 132.3 %copy-start.7 = (bf16[128,1536]{1,0:T(8,128)(2,1)S(1)}, bf16[128,1536]{1,0:T(8,128)(2,1)}, u32[]{:S(2)}) copy-start(bf16[128,1536]{1,0:T(8,128)(2,1)} %param.12) | copy-start | bytes 1179652
  75.6 132.3 %copy-start.8 = (bf16[128,1536]{1,0:T(8,128)(2,1)S(1)}, bf16[128,1536]{1,0:T(8,128)(2,1)}, u32[]{:S(2)}) copy-start(bf16[128,1536]{1,0:T(8,128)(2,1)} %param.13) | copy-start | bytes 1179652
  75.7 324.2 %all-gather.3.cloned.1.call-start = ((), (), s32[]{:S(2)}) async-start(), calls=%async_computation.7 | async-start | bytes 10616832 | tf_op jit(solution)/shard_map/all_gather | solution.py:89
  210.8 228.1 %all-gather.5.cloned.1.call-start = ((), (), s32[]{:S(2)}) async-start(), calls=%async_computation.8 | async-start | bytes 28311552 | tf_op jit(solution)/shard_map/all_gather | solution.py:90
  399.9 1.4 copy-start.3
  402.9 64.0 %all-to-all-start.1 = ((bf16[128,16,384]{0,2,1:T(8,128)(2,1)}), bf16[128,16,384]{0,2,1:T(8,128)(2,1)S(1)}, u32[]{:S(2)}, u32[]{:S(2)}) async-start(bf16[128,16,384]{0,2,1:T(8,128)(2,1)} %bitcast.142), calls=%async_computation.4 | async-start | bytes 3145728 | tf_op jit(solution)/shard_map/all_to_all | solution.py:66
  410.0 134.2 %reduce-scatter.8.cloned.1.call-start = ((), (), s32[]{:S(2)}) async-start(), calls=%async_computation.9 | async-start | bytes 3538944 | tf_op jit(solution)/shard_map/reduce_scatter | solution.py:111
  438.9 9.7 %copy-start.10 = (bf16[2048,3,1536]{2,0,1:T(8,128)(2,1)S(1)}, bf16[2048,3,1536]{2,0,1:T(8,128)(2,1)}, u32[]{:S(2)}) copy-start(bf16[2048,3,1536]{2,0,1:T(8,128)(2,1)} %all-gather.5.cloned.1.call-done) | copy-start | bytes 56623108
  438.9 10.3 %copy-start.11 = (bf16[2,384,1536]{2,1,0:T(8,128)(2,1)S(1)}, bf16[2,384,1536]{2,1,0:T(8,128)(2,1)}, u32[]{:S(2)}) copy-start(bf16[2,384,1536]{2,1,0:T(8,128)(2,1)} %param.15) | copy-start | bytes 7077892
  449.2 5.2 copy-start.12
  468.5 1.7 copy-start.5
  470.2 13.6 %slice-start = ((s8[18874368]{0:T(1024)(128)(4,1)}), s8[4194304]{0:T(1024)(128)(4,1)S(1)}, s32[]{:S(2)}) async-start(s8[18874368]{0:T(1024)(128)(4,1)} %bitcast.152), calls=%async_computation.10 | async-start | bytes 8388608
  470.2 13.6 %slice-start.1 = ((s8[18874368]{0:T(1024)(128)(4,1)}), s8[4194304]{0:T(1024)(128)(4,1)S(1)}, s32[]{:S(2)}) async-start(s8[18874368]{0:T(1024)(128)(4,1)} %bitcast.152), calls=%async_computation.11 | async-start | bytes 8388608
  470.2 13.6 %slice-start.2 = ((s8[18874368]{0:T(1024)(128)(4,1)}), s8[4194304]{0:T(1024)(128)(4,1)S(1)}, s32[]{:S(2)}) async-start(s8[18874368]{0:T(1024)(128)(4,1)} %bitcast.152), calls=%async_computation.12 | async-start | bytes 8388608
  476.8 7.1 %slice-start.3 = ((s8[18874368]{0:T(1024)(128)(4,1)}), s8[4194304]{0:T(1024)(128)(4,1)S(1)}, s32[]{:S(2)}) async-start(s8[18874368]{0:T(1024)(128)(4,1)} %bitcast.152), calls=%async_computation.13 | async-start | bytes 8388608
  476.8 7.1 %slice-start.4 = ((s8[18874368]{0:T(1024)(128)(4,1)}), s8[2097152]{0:T(1024)(128)(4,1)S(1)}, s32[]{:S(2)}) async-start(s8[18874368]{0:T(1024)(128)(4,1)} %bitcast.152), calls=%async_computation.14 | async-start | bytes 4194304
  483.5 1.4 copy-start.6
  492.5 1.9 copy-start.4
  545.9 21.3 %collective-permute-start = (bf16[128,384]{1,0:T(8,128)(2,1)}, bf16[128,384]{1,0:T(8,128)(2,1)}, u32[]{:S(2)}, u32[]{:S(2)}) collective-permute-start(bf16[128,384]{1,0:T(8,128)(2,1)} %get-tuple-element.25), channel_id=1, source_target_pairs={{0,0},{1,32},{2,64},{3,96},{4,8},{5,40},{6,72},{7,104},{8,16},{9,4... | collective-permute-start | bytes 294920 | tf_op jit(solution)/shard_map/ppermute | solution.py:119
  552.1 15.1 %collective-permute-start.1 = (bf16[128,384]{1,0:T(8,128)(2,1)}, bf16[128,384]{1,0:T(8,128)(2,1)}, u32[]{:S(2)}, u32[]{:S(2)}) collective-permute-start(bf16[128,384]{1,0:T(8,128)(2,1)} %get-tuple-element.26), channel_id=1, source_target_pairs={{0,16},{1,48},{2,80},{3,112},{4,24},{5,56},{6,88},{7,120},{8,0},{9... | collective-permute-start | bytes 294920 | tf_op jit(solution)/shard_map/ppermute | solution.py:119
  560.4 8.5 %copy-start.1 = (s32[16]{0:T(128)S(1)}, s32[16]{0:T(128)}, u32[]{:S(2)}) copy-start(s32[16]{0:T(128)} %param.18) | copy-start | bytes 196
Sparse Core Ops, SparseCore 0:
  50.6 24.9 reduce-scatter.3
  78.0 129.8 reduce-scatter.5
  210.9 188.9 all-gather.2
  401.4 37.4 all-gather.4
  467.0 77.1 reduce-scatter.7
where the time goes:
time: 582 us; the launch traced here: 576 us
  waiting for transfers between devices  436 us (75%)
  matrix products  65.2 us (11%)
  starting transfers between devices  25.5 us (4%)
  local copies, waits for them, and re-layouts  24.6 us (4%)
  between operations  15 us (3%)
  other arithmetic  9.76 us (2%)
    all_gather x1, waiting for transfers between devices, shards(): packed = lax.all_gather(packed, CHIPS, axis=0, tiled=True)  189 us
    reduce_scatter x1, waiting for transfers between devices, shards(): lax.psum_scatter(result, CHIPS, scatter_dimension=0, tiled=True)  132 us
    reduce_scatter x1, waiting for transfers between devices, shards(): lax.psum_scatter(partial_rows.reshape(N_TP, row_count // N_TP, width), TP...  41.4 us
    dot_general x6, matrix products, contract_cols(): lax.dot_general(left_op, right_op, (((1,), (1,)), ((), ())), preferred_el...  36 us
    dot_general x6, matrix products, contract_rows(): lax.dot_general(left_op, right_op, (((0,), (0,)), ((), ())), preferred_el...  29.2 us
    all_gather x1, waiting for transfers between devices, shards(): packed = lax.all_gather(packed, 'core', axis=0, tiled=True)  28.3 us
    reduce_scatter x1, waiting for transfers between devices, shards(): lax.psum_scatter(result.reshape(2, row_count // 2, ff), 'core', scatter_d...  25.1 us
    all_to_all x1, waiting for transfers between devices, shards(): lax.all_to_all(out_grad, DP, split_axis=1, concat_axis=0, tiled=True)  20.2 us
  transfers between devices with their start and end apart: 9, of which 6 were waited for; matrix products, arithmetic and copies ran while one was open for 13% of the time, Pallas kernels for 0%

commit v1 on v0

--- a/solution.py
+++ b/solution.py
@@ -61,7 +61,10 @@
     expert_count = w_gate.shape[0]
     ff = gate_pre.shape[1]
     dy_cols = to_gathered_order(
-        lax.all_to_all(out_grad, DP, split_axis=1, concat_axis=0, tiled=True)
+        jnp.concatenate(
+            lax.all_to_all(jnp.stack(jnp.split(out_grad, lax.axis_size(DP), axis=1)), DP, 0, 0),
+            axis=0,
+        )
     )
     x_cols = to_gathered_order(lax.all_to_all(rows_in, DP, split_axis=1, concat_axis=0, tiled=True))
     row_count = dy_cols.shape[0]

time: 582 us -> 604 us (1.038)
  local copies, waits for them, and re-layouts: 24.6 us -> 44.8 us
    unnamed x40 -> x54, local copies, waits for them, and re-layouts: 17.1 us -> 37.6 us
  transfers between devices with their start and end apart: 9 -> 9, of which waited for: 6 -> 6; matrix products, arithmetic and copies ran while one was open for 13% -> 12% of each run, Pallas kernels for 0% -> 0%
where the time goes in v1:
time: 604 us; the launch traced here: 597 us
  waiting for transfers between devices  436 us (72%)
  matrix products  65.7 us (11%)
  local copies, waits for them, and re-layouts  44.8 us (7%)
  starting transfers between devices  25.5 us (4%)
  between operations  15 us (2%)
  other arithmetic  9.76 us (2%)
    all_gather x1, waiting for transfers between devices, shards(): packed = lax.all_gather(packed, CHIPS, axis=0, tiled=True)  189 us
    reduce_scatter x1, waiting for transfers between devices, shards(): lax.psum_scatter(result, CHIPS, scatter_dimension=0, tiled=True)  132 us
    reduce_scatter x1, waiting for transfers between devices, shards(): lax.psum_scatter(partial_rows.reshape(N_TP, row_count // N_TP, width), TP...  41.8 us
    unnamed x54, local copies, waits for them, and re-layouts  37.6 us
    dot_general x6, matrix products, contract_cols(): lax.dot_general(left_op, right_op, (((1,), (1,)), ((), ())), preferred_el...  36 us
    dot_general x6, matrix products, contract_rows(): lax.dot_general(left_op, right_op, (((0,), (0,)), ((), ())), preferred_el...  29.7 us
    all_gather x1, waiting for transfers between devices, shards(): packed = lax.all_gather(packed, 'core', axis=0, tiled=True)  28.3 us
    reduce_scatter x1, waiting for transfers between devices, shards(): lax.psum_scatter(result.reshape(2, row_count // 2, ff), 'core', scatter_d...  25.1 us
  transfers between devices with their start and end apart: 9, of which 6 were waited for; matrix products, arithmetic and copies ran while one was open for 12% of the time, Pallas kernels for 0%

profile of v1, /device:TPU:57, one launch (start us, length us, event | category | flops | bytes accessed | tf_op | source)
XLA Modules:
  0.0 596.8 jit_solution(8932131342964880714)
XLA Ops:
  7.2 1.5 bitcast_dynamic-update-slice_fusion.15
  8.7 1.5 bitcast_dynamic-update-slice_fusion.14
  10.3 1.5 bitcast_dynamic-update-slice_fusion.13
  11.8 1.5 bitcast_dynamic-update-slice_fusion.12
  13.4 1.5 bitcast_dynamic-update-slice_fusion.11
  14.9 1.5 bitcast_dynamic-update-slice_fusion.10
  16.4 1.5 bitcast_dynamic-update-slice_fusion.9
  18.0 1.5 bitcast_dynamic-update-slice_fusion.8
  19.5 1.5 bitcast_dynamic-update-slice_fusion.7
  21.1 1.5 bitcast_dynamic-update-slice_fusion.6
  22.6 1.5 bitcast_dynamic-update-slice_fusion.5
  24.2 1.5 bitcast_dynamic-update-slice_fusion.4
  25.7 1.5 bitcast_dynamic-update-slice_fusion.3
  27.2 1.5 bitcast_dynamic-update-slice_fusion.2
  28.8 1.5 bitcast_dynamic-update-slice_fusion.1
  30.3 1.5 bitcast_dynamic-update-slice_fusion
  31.9 6.2 %all-to-all-start = ((bf16[16,128,384]{2,1,0:T(8,128)(2,1)}), bf16[16,128,384]{2,1,0:T(8,128)(2,1)S(1)}, u32[]{:S(2)}, u32[]{:S(2)}) async-start(bf16[16,128,384]{2,1,0:T(8,128)(2,1)} %bitcast_dynamic-update-slice_fusion), calls=%async_computation | async-start | bytes 3145728 | tf_op jit(solution)/shard_map/all_to_all | solution.py:65
  39.3 20.2 %all-to-all-done = bf16[16,128,384]{2,1,0:T(8,128)(2,1)S(1)} async-done(((bf16[16,128,384]{2,1,0:T(8,128)(2,1)}), bf16[16,128,384]{2,1,0:T(8,128)(2,1)S(1)}, u32[]{:S(2)}, u32[]{:S(2)}) %all-to-all-start) | async-done | bytes 1572896 | tf_op jit(solution)/shard_map/all_to_all | solution.py:65
  60.3 1.4 copy-done.2
  61.7 3.5 fusion.77
  65.2 6.6 %convolution_add_fusion = f32[2048,1536]{1,0:T(8,128)} fusion(f32[2048,1536]{1,0:T(8,128)S(1)} %fusion.77, bf16[2048,384]{1,0:T(8,128)(2,1)S(1)} %bitcast.166, bf16[2,1536,384]{2,1,0:T(8,128)(2,1)S(1)} %copy-done.2), kind=kOutput, calls=%fused_computation.1 | convolution fusion | flops 2419064832 | bytes 27918336 | tf_op jit(solution)/shard_map/dot_general | solution.py:42
  71.8 25.1 %reduce-scatter.4.cloned.1.call-done = f32[1,1024,1536]{2,1,0:T(8,128)} async-done(((f32[2,1024,1536]{2,1,0:T(8,128)}), f32[1,1024,1536]{2,1,0:T(8,128)}) %reduce-scatter.4.cloned.1.call-update) | async-done | bytes 6291472 | tf_op jit(solution)/shard_map/reduce_scatter | solution.py:83
  97.7 131.5 %reduce-scatter.6.cloned.1.call-done = f32[128,1536]{1,0:T(8,128)} async-done(((f32[1024,1536]{1,0:T(8,128)}), f32[128,1536]{1,0:T(8,128)}) %reduce-scatter.6.cloned.1.call-update) | async-done | bytes 786448 | tf_op jit(solution)/shard_map/reduce_scatter | solution.py:86
  229.2 1.7 fusion.97
  232.1 189.0 %all-gather.3.cloned.1.call-done = bf16[1024,3,1536]{2,0,1:T(8,128)(2,1)} async-done(((bf16[128,3,1536]{2,0,1:T(8,128)(2,1)}), bf16[1024,3,1536]{2,0,1:T(8,128)(2,1)}) %all-gather.3.cloned.1.call-update) | async-done | bytes 9437200 | tf_op jit(solution)/shard_map/all_gather | solution.py:92
  421.2 1.4 copy-done.3
  422.6 1.6 copy.32
  424.1 7.1 %all-to-all-start.1 = ((bf16[128,16,384]{0,2,1:T(8,128)(2,1)}), bf16[128,16,384]{0,2,1:T(8,128)(2,1)S(1)}, u32[]{:S(2)}, u32[]{:S(2)}) async-start(bf16[128,16,384]{0,2,1:T(8,128)(2,1)} %bitcast.170), calls=%async_computation.4 | async-start | bytes 3145728 | tf_op jit(solution)/shard_map/all_to_all | solution.py:69
  431.8 28.3 %all-gather.5.cloned.1.call-done = bf16[2048,3,1536]{2,0,1:T(8,128)(2,1)} async-done(((bf16[1024,3,1536]{2,0,1:T(8,128)(2,1)}), bf16[2048,3,1536]{2,0,1:T(8,128)(2,1)}) %all-gather.5.cloned.1.call-update) | async-done | bytes 18874384 | tf_op jit(solution)/shard_map/all_gather | solution.py:93
  460.2 8.4 %fusion.14 = f32[2048,384]{1,0:T(8,128)} fusion(bf16[2048,3,1536]{2,0,1:T(8,128)(2,1)} %all-gather.5.cloned.1.call-done, bf16[2048]{0:T(1024)(128)(2,1)S(1)} %get-tuple-element.32, bf16[2,384,1536]{2,1,0:T(8,128)(2,1)} %param.15), kind=kOutput, calls=%fused_computation.16 | convolution fusion | flops 2419064832 | bytes 10620928 | tf_op jit(solution)/shard_map/dot_general | solution.py:42
  470.5 5.2 fusion.18
  475.6 5.1 fusion.6
  480.8 7.3 %add_add_fusion = f32[2048,384]{1,0:T(8,128)} fusion(f32[2048,384]{1,0:T(8,128)} %fusion.6, f32[2048,384]{1,0:T(8,128)} %fusion.18, f32[2048,384]{1,0:T(8,128)} %fusion.14, bf16[2048,3,1536]{2,0,1:T(8,128)(2,1)S(1)} %copy-done.10, bf16[2048]{0:T(1024)(128)(2,1)S(1)} %get-tuple-element.31, bf16[2,384,1536]{2,1,0:T(8,128)(2,1)S(1)} %copy-done.12), kind=kOutput, calls=%fused_computation.30 | convolution fusion | flops 2421424128 | bytes 20058112 | tf_op jit(solution)/shard_map/dot_general | solution.py:42
  488.0 1.3 copy.35
  490.5 6.9 %fusion.60 = bf16[1,384,1536]{1,2,0:T(8,128)(2,1)S(1)} fusion(bf16[2048,384]{1,0:T(8,128)(2,1)S(1)} %bitcast.174, bf16[2048,3,1536]{2,0,1:T(8,128)(2,1)} %all-gather.5.cloned.1.call-done, bf16[2048]{0:T(1024)(128)(2,1)S(1)} %get-tuple-element.31), kind=kOutput, calls=%fused_computation.49 | convolution fusion | flops 2419654656 | bytes 9048064 | tf_op jit(solution)/shard_map/dot_general | solution.py:36
  497.4 6.8 %fusion.66 = bf16[1,384,1536]{1,2,0:T(8,128)(2,1)S(1)} fusion(bf16[2048,384]{1,0:T(8,128)(2,1)S(1)} %bitcast.175, bf16[2048,3,1536]{2,0,1:T(8,128)(2,1)} %all-gather.5.cloned.1.call-done, bf16[2048]{0:T(1024)(128)(2,1)S(1)} %get-tuple-element.32), kind=kOutput, calls=%fused_computation.51 | convolution fusion | flops 2419654656 | bytes 9048064 | tf_op jit(solution)/shard_map/dot_general | solution.py:36
  505.7 3.7 fusion.63
  509.4 3.9 fusion.69
  513.3 1.7 pad_maximum_fusion
  515.2 3.7 fusion.54
  518.9 4.7 fusion.57
  523.6 41.8 %reduce-scatter.8.cloned.1.call-done = f32[1,256,384]{2,1,0:T(8,128)} async-done(((f32[8,256,384]{2,1,0:T(8,128)}), f32[1,256,384]{2,1,0:T(8,128)}) %reduce-scatter.8.cloned.1.call-update) | async-done | bytes 393232 | tf_op jit(solution)/shard_map/reduce_scatter | solution.py:114
  565.4 1.7 dynamic-slice_bitcast_fusion.1
  567.1 6.2 %collective-permute-start = (bf16[128,384]{1,0:T(8,128)(2,1)}, bf16[128,384]{1,0:T(8,128)(2,1)}, u32[]{:S(2)}, u32[]{:S(2)}) collective-permute-start(bf16[128,384]{1,0:T(8,128)(2,1)} %get-tuple-element.25), channel_id=1, source_target_pairs={{0,0},{1,32},{2,64},{3,96},{4,8},{5,40},{6,72},{7,104},{8,16},{9,4... | collective-permute-start | bytes 294920 | tf_op jit(solution)/shard_map/ppermute | solution.py:122
  573.3 5.3 collective-permute-start.1
  578.6 2.9 pad_maximum_fusion.2
  581.5 2.6 copy.37
  584.1 4.3 copy.36
  (65 shorter events, 10.0 us)
Async XLA Ops:
  7.2 31.0 %copy-start = (s32[16]{0:T(128)S(1)}, s32[16]{0:T(128)}, u32[]{:S(2)}) copy-start(s32[16]{0:T(128)} %param.18) | copy-start | bytes 196
  31.9 6.3 %copy-start.9 = (s32[16]{0:T(128)S(1)}, s32[16]{0:T(128)}, u32[]{:S(2)}) copy-start(s32[16]{0:T(128)} %constant.52) | copy-start | bytes 196
  31.9 27.6 %all-to-all-start = ((bf16[16,128,384]{2,1,0:T(8,128)(2,1)}), bf16[16,128,384]{2,1,0:T(8,128)(2,1)S(1)}, u32[]{:S(2)}, u32[]{:S(2)}) async-start(bf16[16,128,384]{2,1,0:T(8,128)(2,1)} %bitcast_dynamic-update-slice_fusion), calls=%async_computation | async-start | bytes 3145728 | tf_op jit(solution)/shard_map/all_to_all | solution.py:65
  38.1 58.8 %reduce-scatter.4.cloned.1.call-start = ((), (), s32[]{:S(2)}) async-start(), calls=%async_computation.5 | async-start | bytes 18874368 | tf_op jit(solution)/shard_map/reduce_scatter | solution.py:83
  60.1 1.7 copy-start.2
  71.8 157.4 %reduce-scatter.6.cloned.1.call-start = ((), (), s32[]{:S(2)}) async-start(), calls=%async_computation.6 | async-start | bytes 7077888 | tf_op jit(solution)/shard_map/reduce_scatter | solution.py:86
  96.9 132.3 %copy-start.7 = (bf16[128,1536]{1,0:T(8,128)(2,1)S(1)}, bf16[128,1536]{1,0:T(8,128)(2,1)}, u32[]{:S(2)}) copy-start(bf16[128,1536]{1,0:T(8,128)(2,1)} %param.12) | copy-start | bytes 1179652
  96.9 132.3 %copy-start.8 = (bf16[128,1536]{1,0:T(8,128)(2,1)S(1)}, bf16[128,1536]{1,0:T(8,128)(2,1)}, u32[]{:S(2)}) copy-start(bf16[128,1536]{1,0:T(8,128)(2,1)} %param.13) | copy-start | bytes 1179652
  96.9 324.2 %all-gather.3.cloned.1.call-start = ((), (), s32[]{:S(2)}) async-start(), calls=%async_computation.7 | async-start | bytes 10616832 | tf_op jit(solution)/shard_map/all_gather | solution.py:92
  232.1 228.1 %all-gather.5.cloned.1.call-start = ((), (), s32[]{:S(2)}) async-start(), calls=%async_computation.8 | async-start | bytes 28311552 | tf_op jit(solution)/shard_map/all_gather | solution.py:93
  421.2 1.4 copy-start.3
  424.1 65.3 %all-to-all-start.1 = ((bf16[128,16,384]{0,2,1:T(8,128)(2,1)}), bf16[128,16,384]{0,2,1:T(8,128)(2,1)S(1)}, u32[]{:S(2)}, u32[]{:S(2)}) async-start(bf16[128,16,384]{0,2,1:T(8,128)(2,1)} %bitcast.170), calls=%async_computation.4 | async-start | bytes 3145728 | tf_op jit(solution)/shard_map/all_to_all | solution.py:69
  431.3 134.1 %reduce-scatter.8.cloned.1.call-start = ((), (), s32[]{:S(2)}) async-start(), calls=%async_computation.9 | async-start | bytes 3538944 | tf_op jit(solution)/shard_map/reduce_scatter | solution.py:114
  460.2 9.7 %copy-start.10 = (bf16[2048,3,1536]{2,0,1:T(8,128)(2,1)S(1)}, bf16[2048,3,1536]{2,0,1:T(8,128)(2,1)}, u32[]{:S(2)}) copy-start(bf16[2048,3,1536]{2,0,1:T(8,128)(2,1)} %all-gather.5.cloned.1.call-done) | copy-start | bytes 56623108
  460.2 10.3 %copy-start.12 = (bf16[2,384,1536]{2,1,0:T(8,128)(2,1)S(1)}, bf16[2,384,1536]{2,1,0:T(8,128)(2,1)}, u32[]{:S(2)}) copy-start(bf16[2,384,1536]{2,1,0:T(8,128)(2,1)} %param.14) | copy-start | bytes 7077892
  470.5 5.2 copy-start.11
  490.4 7.0 %copy-start.5 = (bf16[2,4,2,128,384]{4,3,2,1,0:T(8,128)(2,1)}, bf16[2,4,2,128,384]{4,3,2,1,0:T(8,128)(2,1)S(1)}, u32[]{:S(2)}) copy-start(bf16[2,4,2,128,384]{4,3,2,1,0:T(8,128)(2,1)S(1)} %copy.34) | copy-start | bytes 4718596
  490.4 14.1 %slice-start = ((s8[18874368]{0:T(1024)(128)(4,1)}), s8[4194304]{0:T(1024)(128)(4,1)S(1)}, s32[]{:S(2)}) async-start(s8[18874368]{0:T(1024)(128)(4,1)} %bitcast.179), calls=%async_computation.10 | async-start | bytes 8388608
  490.4 14.1 %slice-start.1 = ((s8[18874368]{0:T(1024)(128)(4,1)}), s8[4194304]{0:T(1024)(128)(4,1)S(1)}, s32[]{:S(2)}) async-start(s8[18874368]{0:T(1024)(128)(4,1)} %bitcast.179), calls=%async_computation.11 | async-start | bytes 8388608
  490.5 14.1 %slice-start.2 = ((s8[18874368]{0:T(1024)(128)(4,1)}), s8[4194304]{0:T(1024)(128)(4,1)S(1)}, s32[]{:S(2)}) async-start(s8[18874368]{0:T(1024)(128)(4,1)} %bitcast.179), calls=%async_computation.12 | async-start | bytes 8388608
  497.4 7.1 %slice-start.3 = ((s8[18874368]{0:T(1024)(128)(4,1)}), s8[4194304]{0:T(1024)(128)(4,1)S(1)}, s32[]{:S(2)}) async-start(s8[18874368]{0:T(1024)(128)(4,1)} %bitcast.179), calls=%async_computation.13 | async-start | bytes 8388608
  497.4 7.1 %slice-start.4 = ((s8[18874368]{0:T(1024)(128)(4,1)}), s8[2097152]{0:T(1024)(128)(4,1)S(1)}, s32[]{:S(2)}) async-start(s8[18874368]{0:T(1024)(128)(4,1)} %bitcast.179), calls=%async_computation.14 | async-start | bytes 4194304
  504.3 1.4 copy-start.6
  513.3 1.9 copy-start.4
  567.1 21.3 %collective-permute-start = (bf16[128,384]{1,0:T(8,128)(2,1)}, bf16[128,384]{1,0:T(8,128)(2,1)}, u32[]{:S(2)}, u32[]{:S(2)}) collective-permute-start(bf16[128,384]{1,0:T(8,128)(2,1)} %get-tuple-element.25), channel_id=1, source_target_pairs={{0,0},{1,32},{2,64},{3,96},{4,8},{5,40},{6,72},{7,104},{8,16},{9,4... | collective-permute-start | bytes 294920 | tf_op jit(solution)/shard_map/ppermute | solution.py:122
  573.3 15.1 %collective-permute-start.1 = (bf16[128,384]{1,0:T(8,128)(2,1)}, bf16[128,384]{1,0:T(8,128)(2,1)}, u32[]{:S(2)}, u32[]{:S(2)}) collective-permute-start(bf16[128,384]{1,0:T(8,128)(2,1)} %get-tuple-element.26), channel_id=1, source_target_pairs={{0,16},{1,48},{2,80},{3,112},{4,24},{5,56},{6,88},{7,120},{8,0},{9... | collective-permute-start | bytes 294920 | tf_op jit(solution)/shard_map/ppermute | solution.py:122
  584.1 6.0 copy-start.1
Sparse Core Ops, SparseCore 0:
  71.9 24.9 reduce-scatter.3
  99.3 129.8 reduce-scatter.5
  232.2 188.8 all-gather.2
  422.7 37.4 all-gather.4
  488.2 77.2 reduce-scatter.7
